TPU v7x, 512 devices: a whole 4x8x8 slice. The times are simulated.
512 devices in a mesh: dp: 64 (over x, y, core), mp: 8 (over z).
Axes of the slice: x: 4, y: 8, z: 8, core: 2. Of those that a mesh axis runs over, the one named last changes fastest.
Arguments:
- corpus: bfloat16 [8192, 16, 320], P('dp'), may hold values from -6 to 6
- picks: int32 [64, 64], P('dp'), may hold values from 0 to 127
- lengths: int32 [8192], P('dp'), may hold values from 1 to 16, 98304 in all
- langs: int32 [8192], P('dp'), may hold values from 0 to 127
- w_in: bfloat16 [320, 1536], P(None, 'mp'), may hold values from -0.3125 to 0.3125
- lang_table: bfloat16 [128, 1536], P(None, 'mp'), may hold values from -3 to 3
- ln_gain: float32 [1536], P('mp'), may hold values from 0.1 to 1.9
- w_pw1: bfloat16 [1536, 2, 1536], P('dp', None, 'mp'), may hold values from -0.15625 to 0.15625
- kernel: float32 [31, 1536], P(None, 'mp'), may hold values from -1.5 to 1.5
- bn_gain: float32 [1536], P('mp'), may hold values from 0.1 to 1.9
- bn_bias: float32 [1536], P('mp'), may hold values from -3 to 3
- w_pw2: bfloat16 [1536, 1536], P('dp', 'mp'), may hold values from -0.15625 to 0.15625
- cotangent: bfloat16 [65536, 1536], P('dp', 'mp'), may hold values from -6 to 6
Outputs:
- encoded: bfloat16 [65536, 1536], P('dp', 'mp')
- grad_pw1: float32 [1536, 2, 1536], P('dp', None, 'mp')
- grad_pw2: float32 [1536, 1536], P('dp', 'mp')
- grad_kernel: float32 [31, 1536], P(None, 'mp')
- grad_bn_gain: float32 [1536], P('mp')
- grad_bn_bias: float32 [1536], P('mp')
Inputs may be any that keep to these rules, and one draw needn't show every extreme that they name: `picks`: each trainer takes one block of every shard; a shard may give the same block to several trainers.
All inputs are finite; a program needn't handle non-finite values. No bound on the sum of `lengths` on one device may be relied on, other than what follows from the above.
Results may differ from a plain program's by a relative error of at most 0.0057.
Values may be sent and summed in bfloat16 or wider, within the bound.
No kernel may reach another device: no remote copies, remote signals or barrier semaphores. Data moves between devices by JAX's collectives and lax.ppermute only.
A program may use at most 64 MiB of HBM per device.

v0:
```python
import jax
import jax.numpy as jnp
from jax import lax
from jax.sharding import Mesh, PartitionSpec as P

EPS = 1e-05


def depth_conv(values, taps, frames):
    chans = values.shape[1]
    shaped = values.reshape(-1, frames, chans)
    margin = taps.shape[0] // 2
    padded = jnp.pad(shaped, ((0, 0), (margin, margin), (0, 0)))
    total = jnp.zeros(shaped.shape, jnp.float32)
    for step in range(taps.shape[0]):
        total = total + taps[step] * padded[:, step : step + frames]
    return total.reshape(values.shape)


def depth_back(grads, taps, frames):
    chans = grads.shape[1]
    shaped = grads.reshape(-1, frames, chans)
    margin = taps.shape[0] // 2
    padded = jnp.pad(shaped, ((0, 0), (margin, margin), (0, 0)))
    total = jnp.zeros(shaped.shape, jnp.float32)
    for step in range(taps.shape[0]):
        begin = 2 * margin - step
        total = total + taps[step] * padded[:, begin : begin + frames]
    return total.reshape(grads.shape)


def kernel_terms(grads, values, width, frames):
    chans = values.shape[1]
    shaped = values.reshape(-1, frames, chans)
    grad_shaped = grads.reshape(-1, frames, chans)
    margin = width // 2
    padded = jnp.pad(shaped, ((0, 0), (margin, margin), (0, 0)))
    rows_out = []
    for step in range(width):
        rows_out.append(jnp.sum(grad_shaped * padded[:, step : step + frames], axis=(0, 1)))
    return jnp.stack(rows_out, 0)


DP_AXES = ("x", "y", "c")


def dp_sum(value):
    for name in reversed(DP_AXES):
        value = lax.psum(value, name)
    return value


def contract_rows(left, right):
    return lax.dot_general(
        left, right, (((0,), (0,)), ((), ())), preferred_element_type=jnp.float32
    )


def on_device(
    corpus,
    picks,
    lengths,
    langs,
    w_in,
    lang_table,
    ln_gain,
    w_pw1,
    kernel,
    bn_gain,
    bn_bias,
    w_pw2,
    cotangent,
):
    model_width = w_pw2.shape[0] * lax.axis_size(DP_AXES)
    chosen = picks[0]
    blocks = jnp.take(corpus, chosen, axis=0)
    lens_send = jnp.take(lengths, chosen)
    lang_send = jnp.take(langs, chosen)
    received, lens, lang = (
        lax.all_to_all(blocks, DP_AXES, split_axis=0, concat_axis=0, tiled=True),
        lax.all_to_all(lens_send, DP_AXES, split_axis=0, concat_axis=0, tiled=True),
        lax.all_to_all(lang_send, DP_AXES, split_axis=0, concat_axis=0, tiled=True),
    )
    frames = received.shape[1]
    valid = (
        (jnp.arange(frames, dtype=jnp.int32)[None, :] < lens[:, None])
        .astype(jnp.float32)
        .reshape(-1)
    )
    valid_col = valid[:, None]
    mel = received.reshape(-1, received.shape[2]) * valid_col.astype(jnp.bfloat16)
    onehot = (lang[:, None] == jnp.arange(lang_table.shape[0], dtype=jnp.int32)[None, :]).astype(
        jnp.bfloat16
    )
    lang_rows = jnp.dot(onehot, lang_table, preferred_element_type=jnp.float32)
    inputs = jnp.dot(mel, w_in, preferred_element_type=jnp.float32) + jnp.repeat(
        lang_rows, frames, axis=0
    )
    row_sum, row_sq = lax.psum((jnp.sum(inputs, 1), jnp.sum(inputs * inputs, 1)), "mp")
    mean = row_sum / model_width
    var = row_sq / model_width - mean * mean
    normed_in = ((inputs - mean[:, None]) * lax.rsqrt(var + EPS)[:, None] * ln_gain).astype(
        jnp.bfloat16
    )
    weights_one = lax.all_gather(w_pw1, DP_AXES, axis=0, tiled=True).reshape(model_width, -1)
    half = weights_one.shape[1] // 2
    normed_full = lax.all_gather(normed_in, "mp", axis=1, tiled=True)
    pre = jnp.dot(normed_full, weights_one, preferred_element_type=jnp.float32)
    linear_part = pre[:, :half]
    gate_part = pre[:, half:]
    gate_sig = jax.nn.sigmoid(gate_part)
    glu_out = linear_part * gate_sig * valid_col
    conv_out = depth_conv(glu_out, kernel, frames)
    sum_conv, sum_sq, count = dp_sum(
        (
            jnp.sum(valid_col * conv_out, 0),
            jnp.sum(valid_col * conv_out * conv_out, 0),
            jnp.sum(valid),
        )
    )
    mu_conv = sum_conv / count
    var_conv = sum_sq / count - mu_conv * mu_conv
    inv_std = lax.rsqrt(var_conv + EPS)
    normed_conv = (conv_out - mu_conv) * inv_std
    act = normed_conv * bn_gain + bn_bias
    act_sig = jax.nn.sigmoid(act)
    hidden = (valid_col * act * act_sig).astype(jnp.bfloat16)
    weights_two = lax.all_gather(w_pw2, DP_AXES, axis=0, tiled=True)
    hidden_full = lax.all_gather(hidden, "mp", axis=1, tiled=True)
    encoded = (
        inputs + jnp.dot(hidden_full, weights_two, preferred_element_type=jnp.float32)
    ).astype(jnp.bfloat16)
    grad_pw2 = lax.psum_scatter(
        contract_rows(hidden_full, cotangent), DP_AXES, scatter_dimension=0, tiled=True
    )
    cot_full = lax.all_gather(cotangent, "mp", axis=1, tiled=True)
    weights_rows = lax.all_to_all(weights_two, "mp", split_axis=0, concat_axis=1, tiled=True)
    dhidden = lax.dot_general(
        cot_full, weights_rows, (((1,), (1,)), ((), ())), preferred_element_type=jnp.float32
    )
    dact = dhidden * valid_col * act_sig * (1.0 + act * (1.0 - act_sig))
    grad_bias, grad_gain = dp_sum((jnp.sum(dact, 0), jnp.sum(dact * normed_conv, 0)))
    dconv = (
        valid_col * inv_std * bn_gain * (dact - grad_bias / count - normed_conv * grad_gain / count)
    )
    grad_kernel = dp_sum(kernel_terms(dconv, glu_out, kernel.shape[0], frames))
    dglu = depth_back(dconv, kernel, frames)
    dlin = dglu * valid_col * gate_sig
    dgate = dglu * valid_col * linear_part * gate_sig * (1.0 - gate_sig)
    dpre = jnp.concatenate([dlin, dgate], 1).astype(jnp.bfloat16)
    grad_pw1 = lax.psum_scatter(
        contract_rows(normed_full, dpre), DP_AXES, scatter_dimension=0, tiled=True
    )
    grad_pw1 = grad_pw1.reshape(grad_pw1.shape[0], 2, half)
    return (encoded, grad_pw1, grad_pw2, grad_kernel, grad_gain, grad_bias)


def dp_shape(mesh):
    along = mesh.devices[:, 0]
    try:
        xs = len({d.coords[0] for d in along})
        ys = len({d.coords[1] for d in along})
    except AttributeError:
        xs, ys = (1, 1)
    cores = mesh.shape["dp"] // (xs * ys)
    return (xs, ys, cores)


def solution(mesh):
    xs, ys, cores = dp_shape(mesh)
    fine = Mesh(mesh.devices.reshape(xs, ys, cores, mesh.shape["mp"]), DP_AXES + ("mp",))
    D = DP_AXES
    return jax.shard_map(
        on_device,
        mesh=fine,
        in_specs=(
            P(D, None, None),
            P(D, None),
            P(D),
            P(D),
            P(None, "mp"),
            P(None, "mp"),
            P("mp"),
            P(D, None, "mp"),
            P(None, "mp"),
            P("mp"),
            P("mp"),
            P(D, "mp"),
            P(D, "mp"),
        ),
        out_specs=(P(D, "mp"), P(D, None, "mp"), P(D, "mp"), P(None, "mp"), P("mp"), P("mp")),
        check_vma=False,
    )
```

profile of v0, /device:TPU:16, one launch (start us, length us, event | category | flops | bytes accessed | tf_op | source)
XLA Modules:
  0.0 642.6 jit_solution(16453349370406005419)
XLA Ops:
  10.7 10.5 %all-to-all-start.1 = ((s32[64,1,1]{2,1,0:T(1,128)}), s32[64,1,1]{2,1,0:T(1,128)S(1)}, u32[]{:S(2)}, u32[]{:S(2)}) async-start(s32[64,1,1]{2,1,0:T(1,128)} %copy.39), calls=%async_computation.1 | async-start | bytes 65536 | tf_op jit(solution)/shard_map/all_to_all | solution.py:81
  28.8 8.4 %all-to-all-start.2 = ((s32[64,1,1]{2,1,0:T(1,128)}), s32[64,1,1]{2,1,0:T(1,128)S(1)}, u32[]{:S(2)}, u32[]{:S(2)}) async-start(s32[64,1,1]{2,1,0:T(1,128)} %copy.40), calls=%async_computation.2 | async-start | bytes 65536 | tf_op jit(solution)/shard_map/all_to_all | solution.py:82
  38.2 6.6 %all-to-all-done.2 = s32[64,1,1]{2,1,0:T(1,128)S(1)} async-done(((s32[64,1,1]{2,1,0:T(1,128)}), s32[64,1,1]{2,1,0:T(1,128)S(1)}, u32[]{:S(2)}, u32[]{:S(2)}) %all-to-all-start.2) | async-done | bytes 288 | tf_op jit(solution)/shard_map/all_to_all | solution.py:82
  44.9 6.3 all-to-all-start
  55.3 18.0 %all-to-all-done = bf16[64,16,320]{2,1,0:T(8,128)(2,1)S(1)} async-done(((bf16[64,16,320]{2,1,0:T(8,128)(2,1)}), bf16[64,16,320]{2,1,0:T(8,128)(2,1)S(1)}, u32[]{:S(2)}, u32[]{:S(2)}) %all-to-all-start) | async-done | bytes 655392 | tf_op jit(solution)/shard_map/all_to_all | solution.py:80
  73.9 23.5 %all-reduce.3 = (f32[1024]{0:T(1024)S(1)}, f32[1024]{0:T(1024)S(1)}) all-reduce(f32[1024]{0:T(1024)S(1)} %get-tuple-element.42, f32[1024]{0:T(1024)S(1)} %get-tuple-element.41), channel_id=1, replica_groups=mesh['x'=4,'y'=8,'c'=2,'mp'=8] {'mp'}, use_global_device_ids=true, to_apply=%region_3.5 | all-reduce | flops 2048 | bytes 16384 | tf_op jit(solution)/shard_map/psum | solution.py:99
  99.1 52.7 %all_gather.18 = bf16[1536,192]{1,0:T(8,128)(2,1)} all-gather(bf16[24,192]{1,0:T(8,128)(2,1)S(1)} %copy-done.11), channel_id=1, replica_groups=mesh['x'=4,'y'=8,'c'=2,'mp'=8] {'x','y','c'}, dimensions={0}, use_global_device_ids=true | all-gather | bytes 599040 | tf_op jit(solution)/shard_map/all_gather | solution.py:128
  151.7 3.5 all-to-all-start.3
  157.5 29.9 %all-to-all-done.3 = bf16[8,192,192]{2,1,0:T(8,128)(2,1)S(1)} async-done(((bf16[8,192,192]{2,1,0:T(8,128)(2,1)}), bf16[8,192,192]{2,1,0:T(8,128)(2,1)S(1)}, u32[]{:S(2)}, u32[]{:S(2)}) %all-to-all-start.3) | async-done | bytes 589856 | tf_op jit(solution)/shard_map/all_to_all | solution.py:137
  189.3 4.9 copy.42
  194.2 12.3 %all-gather.5.cloned.1.call-done = bf16[1024,1536]{0,1:T(8,128)(2,1)} async-done(((bf16[1024,192]{0,1:T(8,128)(2,1)}), bf16[1024,1536]{0,1:T(8,128)(2,1)}) %all-gather.5.cloned.1.call-update) | async-done | bytes 3145744 | tf_op jit(solution)/shard_map/all_gather | solution.py:107
  206.5 3.6 fusion.82
  210.7 6.3 fusion.3
  218.6 3.2 all-reduce.9
  221.7 15.9 %all-reduce.5 = (f32[192]{0:T(256)}, f32[]{:T(128)}, f32[192]{0:T(256)}) all-reduce(f32[192]{0:T(256)} %get-tuple-element.57, f32[]{:T(128)} %get-tuple-element.58, f32[192]{0:T(256)} %get-tuple-element.59), channel_id=1, replica_groups=mesh['x'=4,'y'=8,'c'=2,'mp'=8] {'y'}, use_global_device_ids=true, to_apply=%region_6.8 | all-reduce | flops 385 | bytes 3080 | tf_op jit(solution)/shard_map/psum | solution.py:49
  237.7 10.5 %all-reduce.7 = (f32[192]{0:T(256)}, f32[]{:T(128)}, f32[192]{0:T(256)}) all-reduce(f32[192]{0:T(256)} %get-tuple-element.47, f32[]{:T(128)} %get-tuple-element.48, f32[192]{0:T(256)} %get-tuple-element.49), channel_id=1, replica_groups=mesh['x'=4,'y'=8,'c'=2,'mp'=8] {'x'}, use_global_device_ids=true, to_apply=%region_7.9 | all-reduce | flops 385 | bytes 3080 | tf_op jit(solution)/shard_map/psum | solution.py:49
  250.1 4.0 all-gather.11.cloned.1.call-done
  254.1 4.5 fusion.77
  258.7 3.1 all-reduce.8
  261.8 15.5 %all-reduce.4 = (f32[192]{0:T(256)}, f32[192]{0:T(256)}) all-reduce(f32[192]{0:T(256)} %get-tuple-element.55, f32[192]{0:T(256)} %get-tuple-element.56), channel_id=1, replica_groups=mesh['x'=4,'y'=8,'c'=2,'mp'=8] {'y'}, use_global_device_ids=true, to_apply=%region_22.24 | all-reduce | flops 384 | bytes 3072 | tf_op jit(solution)/shard_map/psum | solution.py:49
  277.3 11.1 %all-reduce.6 = (f32[192]{0:T(256)}, f32[192]{0:T(256)}) all-reduce(f32[192]{0:T(256)} %get-tuple-element.45, f32[192]{0:T(256)} %get-tuple-element.46), channel_id=1, replica_groups=mesh['x'=4,'y'=8,'c'=2,'mp'=8] {'x'}, use_global_device_ids=true, to_apply=%region_23.25 | all-reduce | flops 384 | bytes 3072 | tf_op jit(solution)/shard_map/psum | solution.py:49
  289.7 4.1 multiply_reduce_fusion.31
  295.4 4.3 fusion.55
  303.6 3.2 fusion.67
  307.1 31.1 %all-gather.9.cloned.1.call-done = bf16[1024,1536]{0,1:T(8,128)(2,1)} async-done(((bf16[1024,192]{0,1:T(8,128)(2,1)}), bf16[1024,1536]{0,1:T(8,128)(2,1)}) %all-gather.9.cloned.1.call-update) | async-done | bytes 3145744 | tf_op jit(solution)/shard_map/all_gather | solution.py:129
  338.2 4.0 fusion.81
  347.0 3.4 psum.157
  350.5 27.6 %psum.158 = f32[31,192]{1,0:T(8,128)S(1)} all-reduce(f32[31,192]{1,0:T(8,128)S(1)} %psum.157), channel_id=1, replica_groups=mesh['x'=4,'y'=8,'c'=2,'mp'=8] {'y'}, use_global_device_ids=true, to_apply=%region_58.60 | all-reduce | flops 5952 | bytes 47616 | tf_op jit(solution)/shard_map/psum | solution.py:49
  378.0 17.6 %psum.159 = f32[31,192]{1,0:T(8,128)} all-reduce(f32[31,192]{1,0:T(8,128)S(1)} %psum.158), channel_id=1, replica_groups=mesh['x'=4,'y'=8,'c'=2,'mp'=8] {'x'}, use_global_device_ids=true, to_apply=%region_59.61 | all-reduce | flops 5952 | bytes 47616 | tf_op jit(solution)/shard_map/psum | solution.py:49
  395.6 87.4 %reduce-scatter.7.cloned.1.call-done = f32[24,384]{1,0:T(8,128)} async-done(((f32[1536,384]{1,0:T(8,128)}), f32[24,384]{1,0:T(8,128)}) %reduce-scatter.7.cloned.1.call-update) | async-done | bytes 36880
  484.5 3.7 fusion.2
  488.2 147.6 %reduce-scatter.5.cloned.1.call-done = f32[24,192]{1,0:T(8,128)} async-done(((f32[1536,192]{1,0:T(8,128)}), f32[24,192]{1,0:T(8,128)}) %reduce-scatter.5.cloned.1.call-update) | async-done | bytes 18448 | tf_op jit(solution)/shard_map/reduce_scatter | solution.py:133
  (86 shorter events, 39.8 us)
Async XLA Ops:
  7.2 66.3 %copy-start = (bf16[320,192]{0,1:T(8,128)(2,1)S(1)}, bf16[320,192]{0,1:T(8,128)(2,1)}, u32[]{:S(2)}) copy-start(bf16[320,192]{0,1:T(8,128)(2,1)} %param.19) | copy-start | bytes 368644
  10.7 18.1 %all-to-all-start.1 = ((s32[64,1,1]{2,1,0:T(1,128)}), s32[64,1,1]{2,1,0:T(1,128)S(1)}, u32[]{:S(2)}, u32[]{:S(2)}) async-start(s32[64,1,1]{2,1,0:T(1,128)} %copy.39), calls=%async_computation.1 | async-start | bytes 65536 | tf_op jit(solution)/shard_map/all_to_all | solution.py:81
  25.4 29.2 %copy-start.9 = (bf16[128,192]{0,1:T(8,128)(2,1)S(1)}, bf16[128,192]{0,1:T(8,128)(2,1)}, u32[]{:S(2)}) copy-start(bf16[128,192]{0,1:T(8,128)(2,1)} %param.20) | copy-start | bytes 147460
  28.8 16.1 %all-to-all-start.2 = ((s32[64,1,1]{2,1,0:T(1,128)}), s32[64,1,1]{2,1,0:T(1,128)S(1)}, u32[]{:S(2)}, u32[]{:S(2)}) async-start(s32[64,1,1]{2,1,0:T(1,128)} %copy.40), calls=%async_computation.2 | async-start | bytes 65536 | tf_op jit(solution)/shard_map/all_to_all | solution.py:82
  44.9 28.4 %all-to-all-start = ((bf16[64,16,320]{2,1,0:T(8,128)(2,1)}), bf16[64,16,320]{2,1,0:T(8,128)(2,1)S(1)}, u32[]{:S(2)}, u32[]{:S(2)}) async-start(bf16[64,16,320]{2,1,0:T(8,128)(2,1)} %broadcast_select_fusion), calls=%async_computation | async-start | bytes 1572864 | tf_op jit(solution)/shard_map/all_to_all | solution.py:80
  51.2 138.1 %all-gather.7.cloned.1.call-start = ((), (), s32[]{:S(2)}) async-start(), calls=%async_computation.7 | async-start | bytes 1597440 | tf_op jit(solution)/shard_map/all_gather | solution.py:105
  52.0 154.6 %all-gather.5.cloned.1.call-start = ((), (), s32[]{:S(2)}) async-start(), calls=%async_computation.6 | async-start | bytes 3538944 | tf_op jit(solution)/shard_map/all_gather | solution.py:107
  53.3 1.3 copy-start.5
  53.4 1.2 copy-start.6
  54.9 42.5 %copy-start.13 = (f32[192]{0:T(256)S(1)}, f32[192]{0:T(256)}, u32[]{:S(2)}) copy-start(f32[192]{0:T(256)} %param.21) | copy-start | bytes 2308
  55.3 43.8 %copy-start.11 = (bf16[24,192]{1,0:T(8,128)(2,1)S(1)}, bf16[24,192]{1,0:T(8,128)(2,1)}, u32[]{:S(2)}) copy-start(bf16[24,192]{1,0:T(8,128)(2,1)} %param.26) | copy-start | bytes 27652
  73.5 82.0 %copy-start.10 = (f32[31,192]{1,0:T(8,128)S(1)}, f32[31,192]{1,0:T(8,128)}, u32[]{:S(2)}) copy-start(f32[31,192]{1,0:T(8,128)} %param.23) | copy-start | bytes 71428
  73.9 115.4 %copy-start.2 = (f32[1024,192]{0,1:T(8,128)}, f32[1024,192]{0,1:T(8,128)S(1)}, u32[]{:S(2)}) copy-start(f32[1024,192]{0,1:T(8,128)S(1)} %get-tuple-element.103) | copy-start | bytes 2359300
  98.3 155.8 %all-gather.11.cloned.1.call-start = ((), (), s32[]{:S(2)}) async-start(), calls=%async_computation.9 | async-start | bytes 3538944 | tf_op jit(solution)/shard_map/all_gather | solution.py:136
  151.7 35.6 %all-to-all-start.3 = ((bf16[8,192,192]{2,1,0:T(8,128)(2,1)}), bf16[8,192,192]{2,1,0:T(8,128)(2,1)S(1)}, u32[]{:S(2)}, u32[]{:S(2)}) async-start(bf16[8,192,192]{2,1,0:T(8,128)(2,1)} %bitcast.41), calls=%async_computation.3 | async-start | bytes 1572864 | tf_op jit(solution)/shard_map/all_to_all | solution.py:137
  155.3 182.9 %all-gather.9.cloned.1.call-start = ((), (), s32[]{:S(2)}) async-start(), calls=%async_computation.8 | async-start | bytes 3538944 | tf_op jit(solution)/shard_map/all_gather | solution.py:129
  206.5 3.6 copy-start.7
  210.2 83.6 %copy-start.1 = (f32[1024,384]{0,1:T(8,128)}, f32[1024,384]{0,1:T(8,128)S(1)}, u32[]{:S(2)}) copy-start(f32[1024,384]{0,1:T(8,128)S(1)} %fusion.82) | copy-start | bytes 4718596
  293.8 7.2 %copy-start.8 = (f32[1024]{0:T(1024)S(1)}, f32[1024]{0:T(1024)}, u32[]{:S(2)}) copy-start(f32[1024]{0:T(1024)} %copy-done.6) | copy-start | bytes 12292
  293.8 189.2 %reduce-scatter.7.cloned.1.call-start = ((), (), s32[]{:S(2)}) async-start(), calls=%async_computation.11 | async-start | bytes 2396160
  301.0 2.6 copy-start.14
  303.6 34.6 %copy-start.4 = (bf16[1024,192]{0,1:T(8,128)(2,1)S(1)}, bf16[1024,192]{0,1:T(8,128)(2,1)}, u32[]{:S(2)}) copy-start(bf16[1024,192]{0,1:T(8,128)(2,1)} %param.27) | copy-start | bytes 1179652
  306.8 328.9 %reduce-scatter.5.cloned.1.call-start = ((), (), s32[]{:S(2)}) async-start(), calls=%async_computation.10 | async-start | bytes 1597440 | tf_op jit(solution)/shard_map/reduce_scatter | solution.py:133
  342.2 4.7 copy-start.12
  342.2 142.3 %copy-start.3 = (f32[1024,192]{0,1:T(8,128)S(1)}, f32[1024,192]{0,1:T(8,128)}, u32[]{:S(2)}) copy-start(f32[1024,192]{0,1:T(8,128)} %copy-done.2) | copy-start | bytes 2359300
Sparse Core Ops, SparseCore 0:
  55.4 86.5 all-gather.6
  144.6 61.8 all-gather.4
  208.6 45.4 all-gather.10
  294.0 44.1 all-gather.8
  342.8 140.2 reduce-scatter.6
  488.1 147.6 reduce-scatter.4
where the time goes:
time: 644 us; the launch traced here: 643 us
  waiting for transfers between devices  340 us (53%)
  blocking collectives  184 us (29%)
  other arithmetic  32.3 us (5%)
  starting transfers between devices  29.4 us (5%)
  local copies, waits for them, and re-layouts  22.4 us (3%)
  matrix products  19.7 us (3%)
  between operations  14.4 us (2%)
    reduce_scatter x1, waiting for transfers between devices, on_device(): lax.psum_scatter(contract_rows(hidden_full, cotangent), DP_AXES, scatter_...  148 us
    psum x9, blocking collectives, dp_sum(): value = lax.psum(value, name)  108 us
    unnamed x7, waiting for transfers between devices  88.9 us
    all_gather x1, blocking collectives, on_device(): weights_two = lax.all_gather(w_pw2, DP_AXES, axis=0, tiled=True)  52.7 us
    all_gather x1, waiting for transfers between devices, on_device(): hidden_full = lax.all_gather(hidden, 'mp', axis=1, tiled=True)  31.1 us
    all_to_all x1, waiting for transfers between devices, on_device(): lax.all_to_all(weights_two, 'mp', split_axis=0, concat_axis=1, tiled=True)  29.9 us
    psum x1, blocking collectives, on_device(): lax.psum((jnp.sum(inputs, 1), jnp.sum(inputs * inputs, 1)), 'mp')  23.5 us
    all_to_all x1, waiting for transfers between devices, on_device(): lax.all_to_all(blocks, DP_AXES, split_axis=0, concat_axis=0, tiled=True)  18 us
  transfers between devices with their start and end apart: 10, of which 9 were waited for; matrix products, arithmetic and copies ran while one was open for 9% of the time, Pallas kernels for 0%

commit v1 on v0

--- a/solution.py
+++ b/solution.py
@@ -4,6 +4,13 @@
 from jax.sharding import Mesh, PartitionSpec as P
 
 EPS = 1e-05
+
+
+def tails_step_on(patch, in_dim):
+    patch = jnp.moveaxis(patch, 0, in_dim)
+    front = patch.shape
+    u_next = patch.reshape(*front[:in_dim], front[in_dim] * front[in_dim + 1], *front[in_dim + 2 :])
+    return u_next
 
 
 def depth_conv(values, taps, frames):
@@ -71,6 +78,29 @@
     w_pw2,
     cotangent,
 ):
+
+    def search_keys(local, peer_axis, along_dim):
+        fan = lax.axis_size(peer_axis)
+        in_order = [(dd, (dd + 1) % fan) for dd in range(fan)]
+        opened, item_now = ([], [])
+        all_blocks = [(ix, j0) for j0, ix in in_order]
+        for to_i in [*range(fan - 1)]:
+            if to_i % 2 == 0:
+                opened.append(
+                    lax.ppermute(
+                        opened[-1] if opened else local, axis_name=peer_axis, perm=in_order
+                    )
+                )
+            else:
+                item_now.append(
+                    lax.ppermute(item_now[-1] if item_now else local, peer_axis, perm=all_blocks)
+                )
+        outer = jnp.stack([*opened[::-1], local, *item_now], axis=0)
+        r1 = lax.axis_index(peer_axis) - len(opened)
+        outer = outer[(jnp.arange(fan) - r1) % fan]
+        part_now = tails_step_on(outer, along_dim)
+        return part_now
+
     model_width = w_pw2.shape[0] * lax.axis_size(DP_AXES)
     chosen = picks[0]
     blocks = jnp.take(corpus, chosen, axis=0)
@@ -126,7 +156,7 @@
     act_sig = jax.nn.sigmoid(act)
     hidden = (valid_col * act * act_sig).astype(jnp.bfloat16)
     weights_two = lax.all_gather(w_pw2, DP_AXES, axis=0, tiled=True)
-    hidden_full = lax.all_gather(hidden, "mp", axis=1, tiled=True)
+    hidden_full = search_keys(hidden, "mp", 1)
     encoded = (
         inputs + jnp.dot(hidden_full, weights_two, preferred_element_type=jnp.float32)
     ).astype(jnp.bfloat16)

time: 644 us -> 608 us (0.944)
  waiting for transfers between devices: 340 us -> 263 us
  starting transfers between devices: 29.4 us -> 53.2 us
  local copies, waits for them, and re-layouts: 22.4 us -> 40.4 us
    unnamed x7 -> x6, waiting for transfers between devices: 88.9 us -> 19.7 us
    all_gather x1 -> x0, waiting for transfers between devices: 31.1 us -> none  [on_device(): hidden_full = lax.all_gather(hidden, 'mp', axis=1, tiled=True)]
    ppermute x0 -> x7, starting transfers between devices: none -> 24.1 us  [the longest x3 15.7 us: search_keys(): lax.ppermute(item_now[-1] if item_now else local, peer_axis, perm=all_blo...]
    ppermute x0 -> x7, waiting for transfers between devices: none -> 19.9 us  [the longest x4 19.9 us: search_keys(): lax.ppermute(opened[-1] if opened else local, axis_name=peer_axis, perm=i...]
    unnamed x31 -> x51, local copies, waits for them, and re-layouts: 2.66 us -> 14.2 us
  transfers between devices with their start and end apart: 10 -> 16, of which waited for: 9 -> 12; matrix products, arithmetic and copies ran while one was open for 9% -> 11% of each run, Pallas kernels for 0% -> 0%
where the time goes in v1:
time: 608 us; the launch traced here: 607 us
  waiting for transfers between devices  263 us (43%)
  blocking collectives  182 us (30%)
  starting transfers between devices  53.2 us (9%)
  local copies, waits for them, and re-layouts  40.4 us (7%)
  other arithmetic  33.7 us (6%)
  matrix products  19.8 us (3%)
  between operations  14.2 us (2%)
    reduce_scatter x1, waiting for transfers between devices, on_device(): lax.psum_scatter(contract_rows(hidden_full, cotangent), DP_AXES, scatter_...  151 us
    psum x9, blocking collectives, dp_sum(): value = lax.psum(value, name)  107 us
    all_gather x1, blocking collectives, on_device(): weights_two = lax.all_gather(w_pw2, DP_AXES, axis=0, tiled=True)  52.4 us
    all_to_all x1, waiting for transfers between devices, on_device(): lax.all_to_all(weights_two, 'mp', split_axis=0, concat_axis=1, tiled=True)  29.8 us
    psum x1, blocking collectives, on_device(): lax.psum((jnp.sum(inputs, 1), jnp.sum(inputs * inputs, 1)), 'mp')  23.5 us
    ppermute x4, waiting for transfers between devices, search_keys(): lax.ppermute(opened[-1] if opened else local, axis_name=peer_axis, perm=i...  19.9 us
    unnamed x6, waiting for transfers between devices  19.7 us
    all_to_all x1, waiting for transfers between devices, on_device(): lax.all_to_all(blocks, DP_AXES, split_axis=0, concat_axis=0, tiled=True)  17.4 us
  transfers between devices with their start and end apart: 16, of which 12 were waited for; matrix products, arithmetic and copies ran while one was open for 11% of the time, Pallas kernels for 0%

profile of v1, /device:TPU:16, one launch (start us, length us, event | category | flops | bytes accessed | tf_op | source)
XLA Modules:
  0.0 606.6 jit_solution(6586741862130417409)
XLA Ops:
  10.7 10.5 %all-to-all-start.1 = ((s32[64,1,1]{2,1,0:T(1,128)}), s32[64,1,1]{2,1,0:T(1,128)S(1)}, u32[]{:S(2)}, u32[]{:S(2)}) async-start(s32[64,1,1]{2,1,0:T(1,128)} %copy.41), calls=%async_computation.1 | async-start | bytes 65536 | tf_op jit(solution)/shard_map/all_to_all | solution.py:111
  28.8 8.4 %all-to-all-start.2 = ((s32[64,1,1]{2,1,0:T(1,128)}), s32[64,1,1]{2,1,0:T(1,128)S(1)}, u32[]{:S(2)}, u32[]{:S(2)}) async-start(s32[64,1,1]{2,1,0:T(1,128)} %copy.42), calls=%async_computation.2 | async-start | bytes 65536 | tf_op jit(solution)/shard_map/all_to_all | solution.py:112
  38.2 6.6 %all-to-all-done.2 = s32[64,1,1]{2,1,0:T(1,128)S(1)} async-done(((s32[64,1,1]{2,1,0:T(1,128)}), s32[64,1,1]{2,1,0:T(1,128)S(1)}, u32[]{:S(2)}, u32[]{:S(2)}) %all-to-all-start.2) | async-done | bytes 288 | tf_op jit(solution)/shard_map/all_to_all | solution.py:112
  44.9 6.3 %all-to-all-start = ((bf16[64,16,320]{2,1,0:T(8,128)(2,1)}), bf16[64,16,320]{2,1,0:T(8,128)(2,1)S(1)}, u32[]{:S(2)}, u32[]{:S(2)}) async-start(bf16[64,16,320]{2,1,0:T(8,128)(2,1)} %broadcast_select_fusion), calls=%async_computation | async-start | bytes 1572864 | tf_op jit(solution)/shard_map/all_to_all | solution.py:110
  55.9 17.4 %all-to-all-done = bf16[64,16,320]{2,1,0:T(8,128)(2,1)S(1)} async-done(((bf16[64,16,320]{2,1,0:T(8,128)(2,1)}), bf16[64,16,320]{2,1,0:T(8,128)(2,1)S(1)}, u32[]{:S(2)}, u32[]{:S(2)}) %all-to-all-start) | async-done | bytes 655392 | tf_op jit(solution)/shard_map/all_to_all | solution.py:110
  73.9 23.5 %all-reduce.3 = (f32[1024]{0:T(1024)S(1)}, f32[1024]{0:T(1024)S(1)}) all-reduce(f32[1024]{0:T(1024)S(1)} %get-tuple-element.42, f32[1024]{0:T(1024)S(1)} %get-tuple-element.41), channel_id=1, replica_groups=mesh['x'=4,'y'=8,'c'=2,'mp'=8] {'mp'}, use_global_device_ids=true, to_apply=%region_3.5 | all-reduce | flops 2048 | bytes 16384 | tf_op jit(solution)/shard_map/psum | solution.py:129
  99.1 52.4 %all_gather.14 = bf16[1536,192]{1,0:T(8,128)(2,1)} all-gather(bf16[24,192]{1,0:T(8,128)(2,1)S(1)} %copy-done.14), channel_id=1, replica_groups=mesh['x'=4,'y'=8,'c'=2,'mp'=8] {'x','y','c'}, dimensions={0}, use_global_device_ids=true | all-gather | bytes 599040 | tf_op jit(solution)/shard_map/all_gather | solution.py:158
  157.2 29.8 %all-to-all-done.3 = bf16[8,192,192]{2,1,0:T(8,128)(2,1)S(1)} async-done(((bf16[8,192,192]{2,1,0:T(8,128)(2,1)}), bf16[8,192,192]{2,1,0:T(8,128)(2,1)S(1)}, u32[]{:S(2)}, u32[]{:S(2)}) %all-to-all-start.3) | async-done | bytes 589856 | tf_op jit(solution)/shard_map/all_to_all | solution.py:167
  189.0 4.9 copy.44
  193.8 12.4 %all-gather.4.cloned.1.call-done = bf16[1024,1536]{0,1:T(8,128)(2,1)} async-done(((bf16[1024,192]{0,1:T(8,128)(2,1)}), bf16[1024,1536]{0,1:T(8,128)(2,1)}) %all-gather.4.cloned.1.call-update) | async-done | bytes 3145744 | tf_op jit(solution)/shard_map/all_gather | solution.py:137
  210.4 6.3 %fusion.3 = (f32[192]{0:T(256)}, f32[192]{0:T(256)}, f32[64,16,192]{2,1,0:T(8,128)}) fusion(f32[64,16]{1,0:T(8,128)} %copy-done.8, f32[192]{0:T(256)} %bitcast.180, f32[192]{0:T(256)} %bitcast.182, f32[192]{0:T(256)} %bitcast.186, f32[192]{0:T(256)} %bitcast.188, f32[192]{0:T(256)} %bitcast.190, f32[192]{0:T(256)} %bitcast.192, f32[192]{0:T(256)} %bitcast.194, ...), kind=kLoop, calls=%fused_computation.72 | loop fusion | flops 12779136 | bytes 1602304 | tf_op jit(solution)/shard_map/reduce_sum | solution.py:147
  221.4 15.9 %all-reduce.5 = (f32[192]{0:T(256)}, f32[]{:T(128)}, f32[192]{0:T(256)}) all-reduce(f32[192]{0:T(256)} %get-tuple-element.57, f32[]{:T(128)} %get-tuple-element.58, f32[192]{0:T(256)} %get-tuple-element.59), channel_id=1, replica_groups=mesh['x'=4,'y'=8,'c'=2,'mp'=8] {'y'}, use_global_device_ids=true, to_apply=%region_6.8 | all-reduce | flops 385 | bytes 3080 | tf_op jit(solution)/shard_map/psum | solution.py:56
  237.4 10.4 %all-reduce.7 = (f32[192]{0:T(256)}, f32[]{:T(128)}, f32[192]{0:T(256)}) all-reduce(f32[192]{0:T(256)} %get-tuple-element.47, f32[]{:T(128)} %get-tuple-element.48, f32[192]{0:T(256)} %get-tuple-element.49), channel_id=1, replica_groups=mesh['x'=4,'y'=8,'c'=2,'mp'=8] {'x'}, use_global_device_ids=true, to_apply=%region_7.9 | all-reduce | flops 385 | bytes 3080 | tf_op jit(solution)/shard_map/psum | solution.py:56
  249.6 3.9 all-gather.8.cloned.1.call-done
  253.5 4.5 fusion.80
  261.2 15.5 %all-reduce.4 = (f32[192]{0:T(256)}, f32[192]{0:T(256)}) all-reduce(f32[192]{0:T(256)} %get-tuple-element.55, f32[192]{0:T(256)} %get-tuple-element.56), channel_id=1, replica_groups=mesh['x'=4,'y'=8,'c'=2,'mp'=8] {'y'}, use_global_device_ids=true, to_apply=%region_22.24 | all-reduce | flops 384 | bytes 3072 | tf_op jit(solution)/shard_map/psum | solution.py:56
  276.7 11.1 %all-reduce.6 = (f32[192]{0:T(256)}, f32[192]{0:T(256)}) all-reduce(f32[192]{0:T(256)} %get-tuple-element.45, f32[192]{0:T(256)} %get-tuple-element.46), channel_id=1, replica_groups=mesh['x'=4,'y'=8,'c'=2,'mp'=8] {'x'}, use_global_device_ids=true, to_apply=%region_23.25 | all-reduce | flops 384 | bytes 3072 | tf_op jit(solution)/shard_map/psum | solution.py:56
  289.1 4.1 multiply_reduce_fusion.31
  294.7 4.4 fusion.55
  308.6 5.6 collective-permute-done
  316.1 5.3 collective-permute-start.4
  321.5 5.0 collective-permute-done.1
  329.1 5.1 collective-permute-start.5
  334.3 6.7 %collective-permute-done.2 = bf16[1024,192]{0,1:T(8,128)(2,1)} collective-permute-done((bf16[1024,192]{0,1:T(8,128)(2,1)S(1)}, bf16[1024,192]{0,1:T(8,128)(2,1)}, u32[]{:S(2)}, u32[]{:S(2)}) %collective-permute-start.2) | collective-permute-done | bytes 393248 | tf_op jit(solution)/shard_map/ppermute | solution.py:90
  344.2 5.3 collective-permute-start.6
  364.9 4.4 gather_fusion.1
  369.2 4.0 fusion.84
  381.5 28.9 %psum.158 = f32[31,192]{1,0:T(8,128)S(1)} all-reduce(f32[31,192]{1,0:T(8,128)S(1)} %psum.157), channel_id=1, replica_groups=mesh['x'=4,'y'=8,'c'=2,'mp'=8] {'y'}, use_global_device_ids=true, to_apply=%region_58.60 | all-reduce | flops 5952 | bytes 47616 | tf_op jit(solution)/shard_map/psum | solution.py:56
  410.4 15.0 %psum.159 = f32[31,192]{1,0:T(8,128)} all-reduce(f32[31,192]{1,0:T(8,128)S(1)} %psum.158), channel_id=1, replica_groups=mesh['x'=4,'y'=8,'c'=2,'mp'=8] {'x'}, use_global_device_ids=true, to_apply=%region_59.61 | all-reduce | flops 5952 | bytes 47616 | tf_op jit(solution)/shard_map/psum | solution.py:56
  425.4 3.7 fusion.2
  429.0 18.3 %reduce-scatter.7.cloned.1.call-done = f32[24,384]{1,0:T(8,128)} async-done(((f32[1536,384]{1,0:T(8,128)}), f32[24,384]{1,0:T(8,128)}) %reduce-scatter.7.cloned.1.call-update) | async-done | bytes 36880
  448.9 151.2 %reduce-scatter.5.cloned.1.call-done = f32[24,192]{1,0:T(8,128)} async-done(((f32[1536,192]{1,0:T(8,128)}), f32[24,192]{1,0:T(8,128)}) %reduce-scatter.5.cloned.1.call-update) | async-done | bytes 18448 | tf_op jit(solution)/shard_map/reduce_scatter | solution.py:163
  (123 shorter events, 85.7 us)
Async XLA Ops:
  7.2 66.3 %copy-start = (bf16[320,192]{0,1:T(8,128)(2,1)S(1)}, bf16[320,192]{0,1:T(8,128)(2,1)}, u32[]{:S(2)}) copy-start(bf16[320,192]{0,1:T(8,128)(2,1)} %param.19) | copy-start | bytes 368644
  10.7 18.1 %all-to-all-start.1 = ((s32[64,1,1]{2,1,0:T(1,128)}), s32[64,1,1]{2,1,0:T(1,128)S(1)}, u32[]{:S(2)}, u32[]{:S(2)}) async-start(s32[64,1,1]{2,1,0:T(1,128)} %copy.41), calls=%async_computation.1 | async-start | bytes 65536 | tf_op jit(solution)/shard_map/all_to_all | solution.py:111
  25.4 29.8 %copy-start.12 = (bf16[128,192]{0,1:T(8,128)(2,1)S(1)}, bf16[128,192]{0,1:T(8,128)(2,1)}, u32[]{:S(2)}) copy-start(bf16[128,192]{0,1:T(8,128)(2,1)} %param.20) | copy-start | bytes 147460
  28.8 16.1 %all-to-all-start.2 = ((s32[64,1,1]{2,1,0:T(1,128)}), s32[64,1,1]{2,1,0:T(1,128)S(1)}, u32[]{:S(2)}, u32[]{:S(2)}) async-start(s32[64,1,1]{2,1,0:T(1,128)} %copy.42), calls=%async_computation.2 | async-start | bytes 65536 | tf_op jit(solution)/shard_map/all_to_all | solution.py:112
  44.9 28.4 %all-to-all-start = ((bf16[64,16,320]{2,1,0:T(8,128)(2,1)}), bf16[64,16,320]{2,1,0:T(8,128)(2,1)S(1)}, u32[]{:S(2)}, u32[]{:S(2)}) async-start(bf16[64,16,320]{2,1,0:T(8,128)(2,1)} %broadcast_select_fusion), calls=%async_computation | async-start | bytes 1572864 | tf_op jit(solution)/shard_map/all_to_all | solution.py:110
  51.2 137.8 %all-gather.6.cloned.1.call-start = ((), (), s32[]{:S(2)}) async-start(), calls=%async_computation.7 | async-start | bytes 1597440 | tf_op jit(solution)/shard_map/all_gather | solution.py:135
  52.0 154.2 %all-gather.4.cloned.1.call-start = ((), (), s32[]{:S(2)}) async-start(), calls=%async_computation.6 | async-start | bytes 3538944 | tf_op jit(solution)/shard_map/all_gather | solution.py:137
  55.5 41.9 %copy-start.20 = (f32[192]{0:T(256)S(1)}, f32[192]{0:T(256)}, u32[]{:S(2)}) copy-start(f32[192]{0:T(256)} %param.21) | copy-start | bytes 2308
  55.8 43.2 %copy-start.14 = (bf16[24,192]{1,0:T(8,128)(2,1)S(1)}, bf16[24,192]{1,0:T(8,128)(2,1)}, u32[]{:S(2)}) copy-start(bf16[24,192]{1,0:T(8,128)(2,1)} %param.26) | copy-start | bytes 27652
  73.5 81.7 %copy-start.13 = (f32[31,192]{1,0:T(8,128)S(1)}, f32[31,192]{1,0:T(8,128)}, u32[]{:S(2)}) copy-start(f32[31,192]{1,0:T(8,128)} %param.23) | copy-start | bytes 71428
  73.9 115.0 %copy-start.4 = (f32[1024,192]{0,1:T(8,128)}, f32[1024,192]{0,1:T(8,128)S(1)}, u32[]{:S(2)}) copy-start(f32[1024,192]{0,1:T(8,128)S(1)} %get-tuple-element.103) | copy-start | bytes 2359300
  98.3 155.2 %all-gather.8.cloned.1.call-start = ((), (), s32[]{:S(2)}) async-start(), calls=%async_computation.8 | async-start | bytes 3538944 | tf_op jit(solution)/shard_map/all_gather | solution.py:166
  151.4 35.6 %all-to-all-start.3 = ((bf16[8,192,192]{2,1,0:T(8,128)(2,1)}), bf16[8,192,192]{2,1,0:T(8,128)(2,1)S(1)}, u32[]{:S(2)}, u32[]{:S(2)}) async-start(bf16[8,192,192]{2,1,0:T(8,128)(2,1)} %bitcast.52), calls=%async_computation.3 | async-start | bytes 1572864 | tf_op jit(solution)/shard_map/all_to_all | solution.py:167
  155.0 292.4 %reduce-scatter.7.cloned.1.call-start = ((), (), s32[]{:S(2)}) async-start(), calls=%async_computation.10 | async-start | bytes 2396160
  209.9 83.4 %copy-start.1 = (f32[1024,384]{0,1:T(8,128)}, f32[1024,384]{0,1:T(8,128)S(1)}, u32[]{:S(2)}) copy-start(f32[1024,384]{0,1:T(8,128)S(1)} %fusion.85) | copy-start | bytes 4718596
  293.3 7.1 %copy-start.11 = (f32[1024]{0:T(1024)S(1)}, f32[1024]{0:T(1024)}, u32[]{:S(2)}) copy-start(f32[1024]{0:T(1024)} %copy-done.9) | copy-start | bytes 12292
  300.4 4.8 copy-start.21
  302.5 11.7 %collective-permute-start = (bf16[1024,192]{0,1:T(8,128)(2,1)}, bf16[1024,192]{0,1:T(8,128)(2,1)}, u32[]{:S(2)}, u32[]{:S(2)}) collective-permute-start(bf16[1024,192]{0,1:T(8,128)(2,1)} %get-tuple-element.69), channel_id=1, source_target_pairs={{0,1},{1,2},{2,3},{3,4},{4,5},{5,6},{6,7},{7,0},{8,9},{9,10},{10,1... | collective-permute-start | bytes 1179656 | tf_op jit(solution)/shard_map/ppermute | solution.py:90
  305.2 37.7 %copy-start.2 = (f32[64,16,192]{2,1,0:T(8,128)S(1)}, f32[64,16,192]{2,1,0:T(8,128)}, u32[]{:S(2)}) copy-start(f32[64,16,192]{2,1,0:T(8,128)} %get-tuple-element.64) | copy-start | bytes 2359300
  308.5 50.7 %copy-start.15 = (f32[192]{0:T(256)S(1)}, f32[192]{0:T(256)}, u32[]{:S(2)}) copy-start(f32[192]{0:T(256)} %get-tuple-element.62) | copy-start | bytes 2308
  308.5 50.7 %copy-start.16 = (f32[192]{0:T(256)S(1)}, f32[192]{0:T(256)}, u32[]{:S(2)}) copy-start(f32[192]{0:T(256)} %get-tuple-element.63) | copy-start | bytes 2308
  308.5 50.7 %copy-start.17 = (f32[192]{0:T(256)S(1)}, f32[192]{0:T(256)}, u32[]{:S(2)}) copy-start(f32[192]{0:T(256)} %param.25) | copy-start | bytes 2308
  308.5 50.7 %copy-start.18 = (f32[192]{0:T(256)S(1)}, f32[192]{0:T(256)}, u32[]{:S(2)}) copy-start(f32[192]{0:T(256)} %param.24) | copy-start | bytes 2308
  308.5 291.5 %reduce-scatter.5.cloned.1.call-start = ((), (), s32[]{:S(2)}) async-start(), calls=%async_computation.9 | async-start | bytes 1597440 | tf_op jit(solution)/shard_map/reduce_scatter | solution.py:163
  314.2 12.3 %collective-permute-start.1 = (bf16[1024,192]{0,1:T(8,128)(2,1)}, bf16[1024,192]{0,1:T(8,128)(2,1)S(1)}, u32[]{:S(2)}, u32[]{:S(2)}) collective-permute-start(bf16[1024,192]{0,1:T(8,128)(2,1)} %collective-permute-done), channel_id=1, source_target_pairs={{0,1},{1,2},{2,3},{3,4},{4,5},{5,6},{6,7},{7,0},{8,9},{9,10},{10,1... | collective-permute-start | bytes 1179656 | tf_op jit(solution)/shard_map/ppermute | solution.py:90
  316.1 13.0 %collective-permute-start.4 = (bf16[1024,192]{0,1:T(8,128)(2,1)}, bf16[1024,192]{0,1:T(8,128)(2,1)}, u32[]{:S(2)}, u32[]{:S(2)}) collective-permute-start(bf16[1024,192]{0,1:T(8,128)(2,1)} %get-tuple-element.69), channel_id=1, source_target_pairs={{1,0},{2,1},{3,2},{4,3},{5,4},{6,5},{7,6},{0,7},{9,8},{10,9},{11,1... | collective-permute-start | bytes 1179656 | tf_op jit(solution)/shard_map/ppermute | solution.py:96
  327.2 13.7 %collective-permute-start.2 = (bf16[1024,192]{0,1:T(8,128)(2,1)S(1)}, bf16[1024,192]{0,1:T(8,128)(2,1)}, u32[]{:S(2)}, u32[]{:S(2)}) collective-permute-start(bf16[1024,192]{0,1:T(8,128)(2,1)S(1)} %collective-permute-done.1), channel_id=1, source_target_pairs={{0,1},{1,2},{2,3},{3,4},{4,5},{5,6},{6,7},{7,0},{8,9},{9,10},{10,1... | collective-permute-start | bytes 1179656 | tf_op jit(solution)/shard_map/ppermute | solution.py:90
  329.1 15.1 %collective-permute-start.5 = (bf16[1024,192]{0,1:T(8,128)(2,1)}, bf16[1024,192]{0,1:T(8,128)(2,1)}, u32[]{:S(2)}, u32[]{:S(2)}) collective-permute-start(bf16[1024,192]{0,1:T(8,128)(2,1)} %collective-permute-done.4), channel_id=1, source_target_pairs={{1,0},{2,1},{3,2},{4,3},{5,4},{6,5},{7,6},{0,7},{9,8},{10,9},{11,1... | collective-permute-start | bytes 1179656 | tf_op jit(solution)/shard_map/ppermute | solution.py:96
  340.9 11.2 %collective-permute-start.3 = (bf16[1024,192]{0,1:T(8,128)(2,1)}, bf16[1024,192]{0,1:T(8,128)(2,1)}, u32[]{:S(2)}, u32[]{:S(2)}) collective-permute-start(bf16[1024,192]{0,1:T(8,128)(2,1)} %collective-permute-done.2), channel_id=1, source_target_pairs={{0,1},{1,2},{2,3},{3,4},{4,5},{5,6},{6,7},{7,0},{8,9},{9,10},{10,1... | collective-permute-start | bytes 1179656 | tf_op jit(solution)/shard_map/ppermute | solution.py:90
  344.2 15.0 %copy-start.3 = (f32[1,1024,192]{1,2,0:T(8,128)S(1)}, f32[1,1024,192]{1,2,0:T(8,128)}, u32[]{:S(2)}) copy-start(f32[1,1024,192]{1,2,0:T(8,128)} %copy.47) | copy-start | bytes 2359300
  344.2 19.9 %collective-permute-start.6 = (bf16[1024,192]{0,1:T(8,128)(2,1)}, bf16[1024,192]{0,1:T(8,128)(2,1)S(1)}, u32[]{:S(2)}, u32[]{:S(2)}) collective-permute-start(bf16[1024,192]{0,1:T(8,128)(2,1)} %collective-permute-done.5), channel_id=1, source_target_pairs={{1,0},{2,1},{3,2},{4,3},{5,4},{6,5},{7,6},{0,7},{9,8},{10,9},{11,1... | collective-permute-start | bytes 1179656 | tf_op jit(solution)/shard_map/ppermute | solution.py:96
  373.2 52.1 %copy-start.5 = (f32[1024,192]{0,1:T(8,128)S(1)}, f32[1024,192]{0,1:T(8,128)}, u32[]{:S(2)}) copy-start(f32[1024,192]{0,1:T(8,128)} %copy-done.4) | copy-start | bytes 2359300
  (6 other events, 16.3 us)
Sparse Core Ops, SparseCore 0:
  55.4 86.6 all-gather.5
  144.7 61.4 all-gather.3
  208.3 45.2 all-gather.7
  308.6 138.6 reduce-scatter.6
  452.4 147.5 reduce-scatter.4
